TPU v7x, 256 devices: a whole 4x4x8 slice. The times are simulated.
256 devices in a mesh: band: 16 (over y, x), slab: 16 (over z, core).
Axes of the slice: x: 4, y: 4, z: 8, core: 2. Of those that a mesh axis runs over, the one named last changes fastest.
Arguments:
- orbitals: bfloat16 [32, 16777216], P('band', 'slab'), may hold values from -6 to 6
- projectors: bfloat16 [16, 16, 512, 18, 128], P('slab', 'band'), may hold values from -0.5 to 0.5
- piece_block: int32 [16, 16, 512], P('slab', 'band'), may hold values from 0 to 511
- piece_atom: int32 [16, 16, 512], P('slab', 'band'), may hold values from -1 to 1151, as said below
- coupling: float32 [6144, 324], P('slab'), may hold values from -0.6 to 0.6
Outputs:
- applied: bfloat16 [32, 16777216], P('band', 'slab')
Inputs may be any that keep to these rules, and one draw needn't show every extreme that they name: `piece_atom`: each entry is -1 (no atom) or side * 384 + slot with side in 0, 1, 2 and slot < 384: the atom in that slot of the slab side - 1 places away along the slab axis, cyclically. Slabs hold different numbers of atoms and of pieces with an atom.
All inputs are finite; a program needn't handle non-finite values.
Results may differ from a plain program's by a relative error of at most 0.0049.
Values may be sent and summed in bfloat16 or wider, within the bound.
No kernel may reach another device: no remote copies, remote signals or barrier semaphores. Data moves between devices by JAX's collectives and lax.ppermute only.
A program may use at most 128 MiB of HBM per device.

v0:
```python
import jax
import jax.numpy as jnp
from jax import lax
from jax.sharding import PartitionSpec as P

PROJ = 18
BLOCK = 128


def extended(cells, sides, width):
    for axis, dim in sides:
        count = lax.axis_size(axis)
        head = lax.slice_in_dim(cells, 0, width, axis=dim)
        tail = lax.slice_in_dim(cells, cells.shape[dim] - width, cells.shape[dim], axis=dim)
        cells = jnp.concatenate(
            [
                lax.ppermute(tail, axis, [(i, (i + 1) % count) for i in range(count)]),
                cells,
                lax.ppermute(head, axis, [((i + 1) % count, i) for i in range(count)]),
            ],
            axis=dim,
        )
    return cells


def fold_rim(padded):
    return padded[0] + padded[2] + padded[4]


def body(orbitals, projectors, piece_block, piece_atom, coupling):
    slab_waves = lax.all_to_all(orbitals, "band", split_axis=1, concat_axis=0, tiled=True)
    band_count = slab_waves.shape[0]
    blocks = slab_waves.reshape(band_count, -1, BLOCK)
    block_count = blocks.shape[1]
    proj_local = projectors[0, 0]
    index_block = piece_block[0, 0]
    index_atom = piece_atom[0, 0]
    pieces = index_block.shape[0]
    slot_count = coupling.shape[0]
    is_live = index_atom >= 0
    picked = jnp.take(blocks, index_block, axis=1)
    projected = jnp.einsum("pjk,npk->pjn", proj_local, picked, preferred_element_type=jnp.float32)
    target = jnp.where(is_live, index_atom, 3 * slot_count)
    partial_value = jax.ops.segment_sum(
        projected.reshape(pieces, -1), target, num_segments=3 * slot_count + 1
    )
    partial_value = partial_value[: 3 * slot_count].reshape(3, slot_count, -1)
    summed = lax.psum(partial_value, "band")
    summed = fold_rim(extended(summed, (("slab", 0),), 1))[None]
    own_total = summed[0]
    share_rows = own_total.shape[0]
    matrices = coupling.reshape(share_rows, PROJ, PROJ)
    dressed = jnp.einsum(
        "aij,ajn->ain",
        matrices,
        own_total.reshape(share_rows, PROJ, band_count),
        precision=lax.Precision.HIGHEST,
    ).astype(jnp.bfloat16)
    beside_all = extended(dressed[None], (("slab", 0),), 1)
    flat_rows = beside_all.reshape(-1, PROJ, band_count)
    chosen = jnp.take(flat_rows, jnp.where(is_live, index_atom, 0), axis=0)
    chosen = jnp.where(is_live[:, None, None], chosen, jnp.zeros((), jnp.bfloat16))
    spread = jnp.einsum("pjk,pjn->npk", proj_local, chosen, preferred_element_type=jnp.float32)
    result = jnp.zeros((band_count, block_count, BLOCK), jnp.float32).at[:, index_block].add(spread)
    result = result.reshape(band_count, -1).astype(jnp.bfloat16)
    return lax.all_to_all(result, "band", split_axis=0, concat_axis=1, tiled=True)


def solution(mesh):
    placed = (
        P("band", "slab"),
        P("slab", "band", None, None, None),
        P("slab", "band", None),
        P("slab", "band", None),
        P("slab", None),
    )
    return jax.shard_map(
        body, mesh=mesh, in_specs=placed, out_specs=P("band", "slab"), check_vma=False
    )
```

profile of v0, /device:TPU:97, one launch (start us, length us, event | category | flops | bytes accessed | tf_op | source)
XLA Modules:
  0.0 466.2 jit_solution(6507110387990564066)
XLA Ops:
  6.5 0.0 copy-start
  6.5 0.0 copy-start.3
  6.5 0.0 copy-start.2
  6.5 6.9 %all-to-all-start = ((bf16[2,16,65536]{2,0,1:T(2,128)(2,1)}), bf16[2,16,65536]{2,0,1:T(2,128)(2,1)}, u32[]{:S(2)}, u32[]{:S(2)}) async-start(bf16[2,16,65536]{2,0,1:T(2,128)(2,1)} %bitcast.41), calls=%async_computation | async-start | bytes 8388608 | tf_op jit(solution)/shard_map/all_to_all | solution.py:31
  13.5 0.0 all-reduce.2.cloned.1.call-start
  13.5 0.0 copy-done.3
  13.6 0.0 copy-done.2
  13.6 62.3 %all-to-all-done = bf16[2,16,65536]{2,0,1:T(2,128)(2,1)} async-done(((bf16[2,16,65536]{2,0,1:T(2,128)(2,1)}), bf16[2,16,65536]{2,0,1:T(2,128)(2,1)}, u32[]{:S(2)}, u32[]{:S(2)}) %all-to-all-start) | async-done | bytes 4194336 | tf_op jit(solution)/shard_map/all_to_all | solution.py:31
  76.0 11.4 %reshape.116 = bf16[32,512,128]{2,1,0:T(8,128)(2,1)} reshape(bf16[16,2,65536]{2,1,0:T(2,128)(2,1)} %bitcast.7) | data formatting | bytes 8388608 | tf_op jit(solution)/shard_map/reshape | solution.py:33
  87.4 6.8 %copy.103 = bf16[32,512,128]{2,0,1:T(8,128)(2,1)} copy(bf16[32,512,128]{2,1,0:T(8,128)(2,1)} %reshape.116) | data formatting | bytes 8388608 | tf_op jit(solution)/shard_map/reshape | solution.py:33
  94.2 5.4 %gather_fusion = bf16[512,32,128]{2,1,0:T(8,128)(2,1)} fusion(bf16[32,512,128]{2,0,1:T(8,128)(2,1)} %copy.103, s32[1024]{0:T(1024)S(1)} %pad_clamp_fusion.1), kind=kCustom, calls=%fused_computation | custom fusion | bytes 8390656 | tf_op jit(solution)/shard_map/jit(_take)/gather | solution.py:41
  99.6 0.0 copy-done
  99.6 10.9 %fusion.11 = f32[512,18,32]{2,1,0:T(8,128)} fusion(bf16[512,18,128]{2,0,1:T(8,128)(2,1)S(1)} %bitcast.35, bf16[512,32,128]{2,1,0:T(8,128)(2,1)} %gather_fusion, pred[512]{0:T(512)(128)(4,1)S(1)} %compare_and_fusion), kind=kOutput, calls=%fused_computation.16 | convolution fusion | flops 77594624 | bytes 7733760 | tf_op jit(solution)/shard_map/pjk,npk->pjn/dot_general | solution.py:42
  110.5 4.5 copy.105
  115.0 1.5 copy.106
  116.5 6.4 %scatter_custom_fusion = f32[1153,576]{1,0:T(8,128)} fusion(s32[512]{0:T(512)S(1)} %bitcast.48, f32[512,576]{1,0:T(8,128)} %copy.106, f32[]{:T(128)} %constant.12.clone.1), kind=kCustom, calls=%fused_computation.21 | custom fusion | flops 294912 | bytes 2657024 | tf_op jit(solution)/shard_map/scatter-add | solution.py:44
  122.8 3.6 slice.20
  126.5 4.6 copy.107
  131.0 0.0 all-reduce.2.cloned.1.call-update
  131.1 103.1 %all-reduce.2.cloned.1.call-done = f32[3,384,576]{1,2,0:T(8,128)} async-done(((f32[3,384,576]{1,2,0:T(8,128)}), f32[3,384,576]{1,2,0:T(8,128)}) %all-reduce.2.cloned.1.call-update) | async-done | bytes 2654224 | tf_op jit(solution)/shard_map/psum | solution.py:48
  234.2 2.8 fusion.25
  236.9 3.6 collective-permute-start
  240.5 0.0 collective-permute-start.1
  240.6 0.0 copy-done.1
  240.6 0.1 reshape.119
  240.6 3.3 copy.109
  244.0 6.9 %collective-permute-done = f32[1,384,576]{1,2,0:T(8,128)} collective-permute-done((f32[1,384,576]{1,2,0:T(8,128)}, f32[1,384,576]{1,2,0:T(8,128)}, u32[]{:S(2)}, u32[]{:S(2)}) %collective-permute-start) | collective-permute-done | bytes 884768 | tf_op jit(solution)/shard_map/ppermute | solution.py:17
  250.9 3.7 collective-permute-done.1
  254.5 1.8 fusion.21
  256.4 3.4 copy.108
  259.8 11.2 %convert_bitcast_fusion = bf16[1,384,18,32]{3,2,1,0:T(8,128)(2,1)} fusion(f32[384,18,32]{2,1,0:T(8,128)} %copy.108, f32[384,18,18]{2,1,0:T(8,128)} %copy.109), kind=kOutput, calls=%fused_computation.17 | convolution fusion | flops 47996928 | bytes 1824768 | tf_op jit(solution)/shard_map/aij,ajn->ain/dot_general | solution.py:53
  270.9 2.9 copy.110
  273.9 0.0 collective-permute-start.2
  273.9 0.5 collective-permute-start.3
  274.4 4.7 %collective-permute-done.2 = bf16[1,384,18,32]{1,3,2,0:T(8,128)(2,1)} collective-permute-done((bf16[1,384,18,32]{1,3,2,0:T(8,128)(2,1)S(1)}, bf16[1,384,18,32]{1,3,2,0:T(8,128)(2,1)}, u32[]{:S(2)}, u32[]{:S(2)}) %collective-permute-start.2) | collective-permute-done | bytes 442400 | tf_op jit(solution)/shard_map/ppermute | solution.py:17
  279.2 3.6 copy.112
  282.8 0.1 collective-permute-done.3
  282.9 2.6 copy.113
  285.4 6.9 %pad_maximum_fusion = bf16[3,384,18,32]{3,2,1,0:T(8,128)(2,1)} fusion(bf16[1,384,18,32]{3,2,1,0:T(8,128)(2,1)} %copy.113, bf16[1,384,18,32]{3,2,1,0:T(8,128)(2,1)} %convert_bitcast_fusion, bf16[1,384,18,32]{3,2,1,0:T(8,128)(2,1)} %copy.112), kind=kLoop, calls=%fused_computation.4 | loop fusion | flops 1327104 | bytes 2654208 | tf_op jit(solution)/shard_map/concatenate | solution.py:15
  292.3 6.0 %gather_fusion.1 = bf16[512,18,32]{2,1,0:T(8,128)(2,1)} fusion(bf16[1152,18,32]{2,1,0:T(8,128)(2,1)} %bitcast.38, s32[1024]{0:T(1024)S(1)} %pad_clamp_fusion), kind=kCustom, calls=%fused_computation.1 | custom fusion | bytes 1181696 | tf_op jit(solution)/shard_map/jit(_take)/gather | solution.py:61
  298.2 13.1 %fusion.4 = f32[512,32,128]{2,1,0:T(8,128)} fusion(bf16[512,18,128]{2,0,1:T(8,128)(2,1)S(1)} %bitcast.36, bf16[512,18,32]{2,1,0:T(8,128)(2,1)} %gather_fusion.1, pred[512]{0:T(512)(128)(4,1)S(1)} %get-tuple-element.8, pred[512]{0:T(512)(128)(4,1)S(1)} %get-tuple-element.7), kind=kOutput, calls=%fused_computation.9 | convolution fusion | flops 76087296 | bytes 11338752 | tf_op jit(solution)/shard_map/pjk,pjn->npk/dot_general | solution.py:63
  311.3 4.3 broadcast_in_dim.47
  315.6 67.5 %scatter_fusion = f32[32,512,128]{2,0,1:T(8,128)} fusion(f32[32,512,128]{2,0,1:T(8,128)} %broadcast_in_dim.47, s32[512]{0:T(512)S(1)} %bitcast.44, f32[512,32,128]{2,1,0:T(8,128)} %fusion.4), kind=kCustom, calls=%fused_computation.3 | custom fusion | flops 2097152 | bytes 25167872 | tf_op jit(solution)/shard_map/scatter-add | solution.py:64
  383.1 4.4 convert_element_type.15
  387.5 3.6 copy.117
  391.1 10.4 %convert_element_type.16 = bf16[16,2,65536]{2,1,0:T(2,128)(2,1)} reshape(bf16[32,512,128]{2,1,0:T(8,128)(2,1)} %copy.117) | data formatting | bytes 8388608 | tf_op jit(solution)/shard_map/convert_element_type | solution.py:65
  401.5 55.9 %all_to_all.32 = bf16[16,2,65536]{2,1,0:T(2,128)(2,1)S(1)} all-to-all(bf16[16,2,65536]{2,1,0:T(2,128)(2,1)} %convert_element_type.16), channel_id=1, replica_groups=mesh['band'=16,'slab'=16] {'band'}, dimensions={0} | all-to-all | bytes 8388608 | tf_op jit(solution)/shard_map/all_to_all | solution.py:66
  457.4 2.0 copy.128
  (7 shorter events, 0.0 us)
Async XLA Ops:
  6.5 93.1 %copy-start = (bf16[1,1,512,18,128]{4,2,3,1,0:T(8,128)(2,1)S(1)}, bf16[1,1,512,18,128]{4,2,3,1,0:T(8,128)(2,1)}, u32[]{:S(2)}) copy-start(bf16[1,1,512,18,128]{4,2,3,1,0:T(8,128)(2,1)} %param.6) | copy-start | bytes 7077892
  6.5 7.0 %copy-start.3 = (s32[1,1,512]{2,1,0:T(1,128)S(1)}, s32[1,1,512]{2,1,0:T(1,128)}, u32[]{:S(2)}) copy-start(s32[1,1,512]{2,1,0:T(1,128)} %param.7) | copy-start | bytes 6148
  6.5 7.0 %copy-start.2 = (s32[1,1,512]{2,1,0:T(1,128)S(1)}, s32[1,1,512]{2,1,0:T(1,128)}, u32[]{:S(2)}) copy-start(s32[1,1,512]{2,1,0:T(1,128)} %param.8) | copy-start | bytes 6148
  6.5 69.4 %all-to-all-start = ((bf16[2,16,65536]{2,0,1:T(2,128)(2,1)}), bf16[2,16,65536]{2,0,1:T(2,128)(2,1)}, u32[]{:S(2)}, u32[]{:S(2)}) async-start(bf16[2,16,65536]{2,0,1:T(2,128)(2,1)} %bitcast.41), calls=%async_computation | async-start | bytes 8388608 | tf_op jit(solution)/shard_map/all_to_all | solution.py:31
  13.5 220.7 %all-reduce.2.cloned.1.call-start = ((), (), s32[]{:S(2)}) async-start(), calls=%async_computation.2 | async-start | bytes 5308416 | tf_op jit(solution)/shard_map/psum | solution.py:48
  131.0 109.5 %copy-start.1 = (f32[384,324]{0,1:T(8,128)S(1)}, f32[384,324]{0,1:T(8,128)}, u32[]{:S(2)}) copy-start(f32[384,324]{0,1:T(8,128)} %param.9) | copy-start | bytes 1492996
  236.9 13.9 %collective-permute-start = (f32[1,384,576]{1,2,0:T(8,128)}, f32[1,384,576]{1,2,0:T(8,128)}, u32[]{:S(2)}, u32[]{:S(2)}) collective-permute-start(f32[1,384,576]{1,2,0:T(8,128)} %get-tuple-element.5), channel_id=1, source_target_pairs={{0,1},{1,2},{2,3},{3,4},{4,5},{5,6},{6,7},{7,8},{8,9},{9,10},{10,1... | collective-permute-start | bytes 2654216 | tf_op jit(solution)/shard_map/ppermute | solution.py:17
  240.5 14.0 %collective-permute-start.1 = (f32[1,384,576]{1,2,0:T(8,128)}, f32[1,384,576]{1,2,0:T(8,128)}, u32[]{:S(2)}, u32[]{:S(2)}) collective-permute-start(f32[1,384,576]{1,2,0:T(8,128)} %get-tuple-element.6), channel_id=1, source_target_pairs={{1,0},{2,1},{3,2},{4,3},{5,4},{6,5},{7,6},{8,7},{9,8},{10,9},{11,1... | collective-permute-start | bytes 2654216 | tf_op jit(solution)/shard_map/ppermute | solution.py:19
  273.9 5.3 %collective-permute-start.2 = (bf16[1,384,18,32]{1,3,2,0:T(8,128)(2,1)S(1)}, bf16[1,384,18,32]{1,3,2,0:T(8,128)(2,1)}, u32[]{:S(2)}, u32[]{:S(2)}) collective-permute-start(bf16[1,384,18,32]{1,3,2,0:T(8,128)(2,1)S(1)} %copy.110), channel_id=1, source_target_pairs={{0,1},{1,2},{2,3},{3,4},{4,5},{5,6},{6,7},{7,8},{8,9},{9,10},{10,1... | collective-permute-start | bytes 1327112 | tf_op jit(solution)/shard_map/ppermute | solution.py:17
  273.9 9.0 %collective-permute-start.3 = (bf16[1,384,18,32]{1,3,2,0:T(8,128)(2,1)S(1)}, bf16[1,384,18,32]{1,3,2,0:T(8,128)(2,1)S(1)}, u32[]{:S(2)}, u32[]{:S(2)}) collective-permute-start(bf16[1,384,18,32]{1,3,2,0:T(8,128)(2,1)S(1)} %copy.110), channel_id=1, source_target_pairs={{1,0},{2,1},{3,2},{4,3},{5,4},{6,5},{7,6},{8,7},{9,8},{10,9},{11,1... | collective-permute-start | bytes 1327112 | tf_op jit(solution)/shard_map/ppermute | solution.py:19
Sparse Core Ops, SparseCore 0:
  131.2 102.9 all-reduce.1
where the time goes:
time: 468 us; the launch traced here: 466 us
  waiting for transfers between devices  181 us (39%)
  other arithmetic  87 us (19%)
  local copies, waits for them, and re-layouts  82.8 us (18%)
  blocking collectives  55.9 us (12%)
  matrix products  35.1 us (8%)
  between operations  13.5 us (3%)
  starting transfers between devices  11.1 us (2%)
    psum x1, waiting for transfers between devices, body(): summed = lax.psum(partial_value, 'band')  103 us
    scatter-add x1, other arithmetic, body(): jnp.zeros((band_count, block_count, BLOCK), jnp.float32).at[:, index_block]  67.5 us
    all_to_all x1, waiting for transfers between devices, body(): lax.all_to_all(orbitals, 'band', split_axis=1, concat_axis=0, tiled=True)  62.3 us
    all_to_all x1, blocking collectives, body(): lax.all_to_all(result, 'band', split_axis=0, concat_axis=1, tiled=True)  55.9 us
    reshape x2, local copies, waits for them, and re-layouts, body(): blocks = slab_waves.reshape(band_count, -1, BLOCK)  18.2 us
    convert_element_type x2, local copies, waits for them, and re-layouts, body(): result = result.reshape(band_count, -1).astype(jnp.bfloat16)  14 us
    dot_general x1, matrix products, body(): jnp.einsum('pjk,pjn->npk', proj_local, chosen, preferred_element_type=jnp...  13.1 us
    ppermute x2, waiting for transfers between devices, extended(): lax.ppermute(tail, axis, [(i, (i + 1) % count) for i in range(count)])  11.6 us
  transfers between devices with their start and end apart: 6, of which 6 were waited for; matrix products, arithmetic and copies ran while one was open for 2% of the time, Pallas kernels for 0%

commit v1 on v0

--- a/solution.py
+++ b/solution.py
@@ -45,7 +45,9 @@
         projected.reshape(pieces, -1), target, num_segments=3 * slot_count + 1
     )
     partial_value = partial_value[: 3 * slot_count].reshape(3, slot_count, -1)
-    summed = lax.psum(partial_value, "band")
+    summed = partial_value
+    for hop in (1, 2, 4, 8):
+        summed = summed + lax.ppermute(summed, "band", [(dev, dev ^ hop) for dev in range(16)])
     summed = fold_rim(extended(summed, (("slab", 0),), 1))[None]
     own_total = summed[0]
     share_rows = own_total.shape[0]

time: 468 us -> 587 us (1.25)
  waiting for transfers between devices: 181 us -> 304 us
  between operations: 13.5 us -> 0.14 us
  starting transfers between devices: 11.1 us -> 17.4 us
    ppermute x0 -> x4, waiting for transfers between devices: none -> 226 us  [body(): lax.ppermute(summed, 'band', [(dev, dev ^ hop) for dev in range(16)])]
    psum x1 -> x0, waiting for transfers between devices: 103 us -> none  [body(): summed = lax.psum(partial_value, 'band')]
  transfers between devices with their start and end apart: 6 -> 9, of which waited for: 6 -> 9; matrix products, arithmetic and copies ran while one was open for 2% -> 1% of each run, Pallas kernels for 0% -> 0%
where the time goes in v1:
time: 587 us; the launch traced here: 585 us
  waiting for transfers between devices  304 us (52%)
  other arithmetic  89.8 us (15%)
  local copies, waits for them, and re-layouts  83.2 us (14%)
  blocking collectives  55.1 us (9%)
  matrix products  35.1 us (6%)
  starting transfers between devices  17.4 us (3%)
    ppermute x4, waiting for transfers between devices, body(): lax.ppermute(summed, 'band', [(dev, dev ^ hop) for dev in range(16)])  226 us
    scatter-add x1, other arithmetic, body(): jnp.zeros((band_count, block_count, BLOCK), jnp.float32).at[:, index_block]  67.3 us
    all_to_all x1, waiting for transfers between devices, body(): lax.all_to_all(orbitals, 'band', split_axis=1, concat_axis=0, tiled=True)  62.4 us
    all_to_all x1, blocking collectives, body(): lax.all_to_all(result, 'band', split_axis=0, concat_axis=1, tiled=True)  55.1 us
    reshape x2, local copies, waits for them, and re-layouts, body(): blocks = slab_waves.reshape(band_count, -1, BLOCK)  18.2 us
    convert_element_type x2, local copies, waits for them, and re-layouts, body(): result = result.reshape(band_count, -1).astype(jnp.bfloat16)  14.1 us
    dot_general x1, matrix products, body(): jnp.einsum('pjk,pjn->npk', proj_local, chosen, preferred_element_type=jnp...  13 us
  transfers between devices with their start and end apart: 9, of which 9 were waited for; matrix products, arithmetic and copies ran while one was open for 1% of the time, Pallas kernels for 0%

profile of v1, /device:TPU:97, one launch (start us, length us, event | category | flops | bytes accessed | tf_op | source)
XLA Modules:
  0.0 584.7 jit_solution(15468078543818034140)
XLA Ops:
  0.0 6.9 %all-to-all-start = ((bf16[2,16,65536]{2,0,1:T(2,128)(2,1)}), bf16[2,16,65536]{2,0,1:T(2,128)(2,1)}, u32[]{:S(2)}, u32[]{:S(2)}) async-start(bf16[2,16,65536]{2,0,1:T(2,128)(2,1)} %bitcast.41), calls=%async_computation | async-start | bytes 8388608 | tf_op jit(solution)/shard_map/all_to_all | solution.py:31
  7.0 62.4 %all-to-all-done = bf16[2,16,65536]{2,0,1:T(2,128)(2,1)} async-done(((bf16[2,16,65536]{2,0,1:T(2,128)(2,1)}), bf16[2,16,65536]{2,0,1:T(2,128)(2,1)}, u32[]{:S(2)}, u32[]{:S(2)}) %all-to-all-start) | async-done | bytes 4194336 | tf_op jit(solution)/shard_map/all_to_all | solution.py:31
  69.4 11.4 %reshape.116 = bf16[32,512,128]{2,1,0:T(8,128)(2,1)} reshape(bf16[16,2,65536]{2,1,0:T(2,128)(2,1)} %bitcast.7) | data formatting | bytes 8388608 | tf_op jit(solution)/shard_map/reshape | solution.py:33
  80.8 6.8 %copy.135 = bf16[32,512,128]{2,0,1:T(8,128)(2,1)} copy(bf16[32,512,128]{2,1,0:T(8,128)(2,1)} %reshape.116) | data formatting | bytes 8388608 | tf_op jit(solution)/shard_map/reshape | solution.py:33
  87.7 5.4 gather_fusion
  93.1 10.9 %fusion.11 = f32[512,18,32]{2,1,0:T(8,128)} fusion(bf16[512,18,128]{2,0,1:T(8,128)(2,1)S(1)} %bitcast.35, bf16[512,32,128]{2,1,0:T(8,128)(2,1)} %gather_fusion, pred[512]{0:T(512)(128)(4,1)S(1)} %compare_and_fusion), kind=kOutput, calls=%fused_computation.16 | convolution fusion | flops 77594624 | bytes 7733760 | tf_op jit(solution)/shard_map/pjk,npk->pjn/dot_general | solution.py:42
  104.0 4.5 copy.137
  108.5 1.5 copy.138
  110.0 6.5 %scatter_custom_fusion = f32[1153,576]{1,0:T(8,128)} fusion(s32[512]{0:T(512)S(1)} %bitcast.48, f32[512,576]{1,0:T(8,128)} %copy.138, f32[]{:T(128)} %constant.12.clone.1), kind=kCustom, calls=%fused_computation.21 | custom fusion | flops 294912 | bytes 2657024 | tf_op jit(solution)/shard_map/scatter-add | solution.py:44
  116.5 3.6 slice.20
  120.1 4.6 copy.140
  124.7 57.6 %collective-permute-done = f32[3,384,576]{1,2,0:T(8,128)S(1)} collective-permute-done((f32[3,384,576]{1,2,0:T(8,128)}, f32[3,384,576]{1,2,0:T(8,128)S(1)}, u32[]{:S(2)}, u32[]{:S(2)}) %collective-permute-start) | collective-permute-done | bytes 2654240 | tf_op jit(solution)/shard_map/ppermute | solution.py:50
  182.3 2.0 add.79
  184.3 0.7 collective-permute-start.1
  185.0 57.4 %collective-permute-done.1 = f32[3,384,576]{1,2,0:T(8,128)S(1)} collective-permute-done((f32[3,384,576]{1,2,0:T(8,128)S(1)}, f32[3,384,576]{1,2,0:T(8,128)S(1)}, u32[]{:S(2)}, u32[]{:S(2)}) %collective-permute-start.1) | collective-permute-done | bytes 2654240 | tf_op jit(solution)/shard_map/ppermute | solution.py:50
  242.4 0.3 add.80
  242.7 0.1 collective-permute-start.2
  242.8 55.6 %collective-permute-done.2 = f32[3,384,576]{1,2,0:T(8,128)S(1)} collective-permute-done((f32[3,384,576]{1,2,0:T(8,128)S(1)}, f32[3,384,576]{1,2,0:T(8,128)S(1)}, u32[]{:S(2)}, u32[]{:S(2)}) %collective-permute-start.2) | collective-permute-done | bytes 2654240 | tf_op jit(solution)/shard_map/ppermute | solution.py:50
  298.4 0.3 add.81
  298.6 1.7 collective-permute-start.3
  300.3 55.9 %collective-permute-done.3 = f32[3,384,576]{1,2,0:T(8,128)S(1)} collective-permute-done((f32[3,384,576]{1,2,0:T(8,128)S(1)}, f32[3,384,576]{1,2,0:T(8,128)S(1)}, u32[]{:S(2)}, u32[]{:S(2)}) %collective-permute-start.3) | collective-permute-done | bytes 2654240 | tf_op jit(solution)/shard_map/ppermute | solution.py:50
  356.3 0.3 add.82
  356.5 1.5 copy-done.1
  358.0 1.4 fusion.25
  359.4 7.4 %collective-permute-start.4 = (f32[1,384,576]{1,2,0:T(8,128)}, f32[1,384,576]{1,2,0:T(8,128)}, u32[]{:S(2)}, u32[]{:S(2)}) collective-permute-start(f32[1,384,576]{1,2,0:T(8,128)} %get-tuple-element.5), channel_id=1, source_target_pairs={{0,1},{1,2},{2,3},{3,4},{4,5},{5,6},{6,7},{7,8},{8,9},{9,10},{10,1... | collective-permute-start | bytes 2654216 | tf_op jit(solution)/shard_map/ppermute | solution.py:17
  366.8 0.1 reshape.119
  366.9 3.6 copy.142
  370.5 6.7 %collective-permute-done.4 = f32[1,384,576]{1,2,0:T(8,128)} collective-permute-done((f32[1,384,576]{1,2,0:T(8,128)}, f32[1,384,576]{1,2,0:T(8,128)}, u32[]{:S(2)}, u32[]{:S(2)}) %collective-permute-start.4) | collective-permute-done | bytes 884768 | tf_op jit(solution)/shard_map/ppermute | solution.py:17
  377.1 3.7 collective-permute-done.5
  380.8 1.8 fusion.21
  382.6 3.4 copy.141
  386.0 11.2 %convert_bitcast_fusion = bf16[1,384,18,32]{3,2,1,0:T(8,128)(2,1)} fusion(f32[384,18,32]{2,1,0:T(8,128)} %copy.141, f32[384,18,18]{2,1,0:T(8,128)} %copy.142), kind=kOutput, calls=%fused_computation.17 | convolution fusion | flops 47996928 | bytes 1824768 | tf_op jit(solution)/shard_map/aij,ajn->ain/dot_general | solution.py:55
  397.2 2.9 copy.143
  400.2 0.5 collective-permute-start.7
  400.7 4.7 collective-permute-done.6
  405.4 3.7 copy.145
  409.1 0.1 collective-permute-done.7
  409.1 2.5 copy.146
  411.7 6.9 %pad_maximum_fusion = bf16[3,384,18,32]{3,2,1,0:T(8,128)(2,1)} fusion(bf16[1,384,18,32]{3,2,1,0:T(8,128)(2,1)} %copy.146, bf16[1,384,18,32]{3,2,1,0:T(8,128)(2,1)} %convert_bitcast_fusion, bf16[1,384,18,32]{3,2,1,0:T(8,128)(2,1)} %copy.145), kind=kLoop, calls=%fused_computation.4 | loop fusion | flops 1327104 | bytes 2654208 | tf_op jit(solution)/shard_map/concatenate | solution.py:15
  418.5 6.0 %gather_fusion.1 = bf16[512,18,32]{2,1,0:T(8,128)(2,1)} fusion(bf16[1152,18,32]{2,1,0:T(8,128)(2,1)} %bitcast.38, s32[1024]{0:T(1024)S(1)} %pad_clamp_fusion), kind=kCustom, calls=%fused_computation.1 | custom fusion | bytes 1181696 | tf_op jit(solution)/shard_map/jit(_take)/gather | solution.py:63
  424.5 13.0 %fusion.4 = f32[512,32,128]{2,1,0:T(8,128)} fusion(bf16[512,18,128]{2,0,1:T(8,128)(2,1)S(1)} %bitcast.36, bf16[512,18,32]{2,1,0:T(8,128)(2,1)} %gather_fusion.1, pred[512]{0:T(512)(128)(4,1)S(1)} %get-tuple-element.8, pred[512]{0:T(512)(128)(4,1)S(1)} %get-tuple-element.7), kind=kOutput, calls=%fused_computation.9 | convolution fusion | flops 76087296 | bytes 11338752 | tf_op jit(solution)/shard_map/pjk,pjn->npk/dot_general | solution.py:65
  437.5 4.3 broadcast_in_dim.47
  441.8 67.3 %scatter_fusion = f32[32,512,128]{2,0,1:T(8,128)} fusion(f32[32,512,128]{2,0,1:T(8,128)} %broadcast_in_dim.47, s32[512]{0:T(512)S(1)} %bitcast.44, f32[512,32,128]{2,1,0:T(8,128)} %fusion.4), kind=kCustom, calls=%fused_computation.3 | custom fusion | flops 2097152 | bytes 25167872 | tf_op jit(solution)/shard_map/scatter-add | solution.py:66
  509.1 4.4 convert_element_type.15
  513.5 3.6 copy.150
  517.2 10.5 %convert_element_type.16 = bf16[16,2,65536]{2,1,0:T(2,128)(2,1)} reshape(bf16[32,512,128]{2,1,0:T(8,128)(2,1)} %copy.150) | data formatting | bytes 8388608 | tf_op jit(solution)/shard_map/convert_element_type | solution.py:67
  527.6 55.1 %all_to_all.32 = bf16[16,2,65536]{2,1,0:T(2,128)(2,1)S(1)} all-to-all(bf16[16,2,65536]{2,1,0:T(2,128)(2,1)} %convert_element_type.16), channel_id=1, replica_groups=mesh['band'=16,'slab'=16] {'band'}, dimensions={0} | all-to-all | bytes 8388608 | tf_op jit(solution)/shard_map/all_to_all | solution.py:68
  582.7 2.0 copy.160
  (18 shorter events, 0.1 us)
Async XLA Ops:
  0.0 93.1 %copy-start = (bf16[1,1,512,18,128]{4,2,3,1,0:T(8,128)(2,1)S(1)}, bf16[1,1,512,18,128]{4,2,3,1,0:T(8,128)(2,1)}, u32[]{:S(2)}) copy-start(bf16[1,1,512,18,128]{4,2,3,1,0:T(8,128)(2,1)} %param.6) | copy-start | bytes 7077892
  0.0 7.0 %copy-start.4 = (s32[1,1,512]{2,1,0:T(1,128)S(1)}, s32[1,1,512]{2,1,0:T(1,128)}, u32[]{:S(2)}) copy-start(s32[1,1,512]{2,1,0:T(1,128)} %param.7) | copy-start | bytes 6148
  0.0 7.0 %copy-start.3 = (s32[1,1,512]{2,1,0:T(1,128)S(1)}, s32[1,1,512]{2,1,0:T(1,128)}, u32[]{:S(2)}) copy-start(s32[1,1,512]{2,1,0:T(1,128)} %param.8) | copy-start | bytes 6148
  0.0 69.4 %all-to-all-start = ((bf16[2,16,65536]{2,0,1:T(2,128)(2,1)}), bf16[2,16,65536]{2,0,1:T(2,128)(2,1)}, u32[]{:S(2)}, u32[]{:S(2)}) async-start(bf16[2,16,65536]{2,0,1:T(2,128)(2,1)} %bitcast.41), calls=%async_computation | async-start | bytes 8388608 | tf_op jit(solution)/shard_map/all_to_all | solution.py:31
  124.7 57.6 %collective-permute-start = (f32[3,384,576]{1,2,0:T(8,128)}, f32[3,384,576]{1,2,0:T(8,128)S(1)}, u32[]{:S(2)}, u32[]{:S(2)}) collective-permute-start(f32[3,384,576]{1,2,0:T(8,128)} %copy.140), channel_id=1, source_target_pairs={{0,16},{16,0},{32,48},{48,32},{64,80},{80,64},{96,112},{112,96},{1... | collective-permute-start | bytes 7962632 | tf_op jit(solution)/shard_map/ppermute | solution.py:50
  184.3 58.1 %collective-permute-start.1 = (f32[3,384,576]{1,2,0:T(8,128)S(1)}, f32[3,384,576]{1,2,0:T(8,128)S(1)}, u32[]{:S(2)}, u32[]{:S(2)}) collective-permute-start(f32[3,384,576]{1,2,0:T(8,128)S(1)} %add.79), channel_id=1, source_target_pairs={{0,32},{16,48},{32,0},{48,16},{64,96},{80,112},{96,64},{112,80},{1... | collective-permute-start | bytes 7962632 | tf_op jit(solution)/shard_map/ppermute | solution.py:50
  242.7 55.7 %collective-permute-start.2 = (f32[3,384,576]{1,2,0:T(8,128)S(1)}, f32[3,384,576]{1,2,0:T(8,128)S(1)}, u32[]{:S(2)}, u32[]{:S(2)}) collective-permute-start(f32[3,384,576]{1,2,0:T(8,128)S(1)} %add.80), channel_id=1, source_target_pairs={{0,64},{16,80},{32,96},{48,112},{64,0},{80,16},{96,32},{112,48},{1... | collective-permute-start | bytes 7962632 | tf_op jit(solution)/shard_map/ppermute | solution.py:50
  298.6 57.6 %collective-permute-start.3 = (f32[3,384,576]{1,2,0:T(8,128)S(1)}, f32[3,384,576]{1,2,0:T(8,128)S(1)}, u32[]{:S(2)}, u32[]{:S(2)}) collective-permute-start(f32[3,384,576]{1,2,0:T(8,128)S(1)} %add.81), channel_id=1, source_target_pairs={{0,128},{16,144},{32,160},{48,176},{64,192},{80,208},{96,224},{112... | collective-permute-start | bytes 7962632 | tf_op jit(solution)/shard_map/ppermute | solution.py:50
  356.5 1.5 copy-start.1
  358.0 8.8 %copy-start.2 = (f32[384,324]{0,1:T(8,128)S(1)}, f32[384,324]{0,1:T(8,128)}, u32[]{:S(2)}) copy-start(f32[384,324]{0,1:T(8,128)} %param.9) | copy-start | bytes 1492996
  359.4 17.7 %collective-permute-start.4 = (f32[1,384,576]{1,2,0:T(8,128)}, f32[1,384,576]{1,2,0:T(8,128)}, u32[]{:S(2)}, u32[]{:S(2)}) collective-permute-start(f32[1,384,576]{1,2,0:T(8,128)} %get-tuple-element.5), channel_id=1, source_target_pairs={{0,1},{1,2},{2,3},{3,4},{4,5},{5,6},{6,7},{7,8},{8,9},{9,10},{10,1... | collective-permute-start | bytes 2654216 | tf_op jit(solution)/shard_map/ppermute | solution.py:17
  366.8 14.0 %collective-permute-start.5 = (f32[1,384,576]{1,2,0:T(8,128)}, f32[1,384,576]{1,2,0:T(8,128)}, u32[]{:S(2)}, u32[]{:S(2)}) collective-permute-start(f32[1,384,576]{1,2,0:T(8,128)} %get-tuple-element.6), channel_id=1, source_target_pairs={{1,0},{2,1},{3,2},{4,3},{5,4},{6,5},{7,6},{8,7},{9,8},{10,9},{11,1... | collective-permute-start | bytes 2654216 | tf_op jit(solution)/shard_map/ppermute | solution.py:19
  400.1 5.3 collective-permute-start.6
  400.2 9.0 %collective-permute-start.7 = (bf16[1,384,18,32]{1,3,2,0:T(8,128)(2,1)S(1)}, bf16[1,384,18,32]{1,3,2,0:T(8,128)(2,1)S(1)}, u32[]{:S(2)}, u32[]{:S(2)}) collective-permute-start(bf16[1,384,18,32]{1,3,2,0:T(8,128)(2,1)S(1)} %copy.143), channel_id=1, source_target_pairs={{1,0},{2,1},{3,2},{4,3},{5,4},{6,5},{7,6},{8,7},{9,8},{10,9},{11,1... | collective-permute-start | bytes 1327112 | tf_op jit(solution)/shard_map/ppermute | solution.py:19
